TPU v7x, 256 devices: a whole 4x4x8 slice. The times are simulated.
256 devices in a mesh: dp: 32 (over x, y, z_lo), tensor: 8 (over z_hi, core).
Axes of the slice: x: 4, y: 4, z: 8 (z_hi: 4, z_lo: 2; z = z_hi * 2 + z_lo), core: 2. Of those that a mesh axis runs over, the one named last changes fastest.
Arguments:
- arrivals: bfloat16 [32768, 2048], P('dp', 'tensor')
- deal: int32 [32, 32], P('dp'), may hold values from 0 to 1023, as said below
- seg_ids: int32 [32, 1024], P('dp'), may hold values from 0 to 7, never falling along the last dimension, each value on 1 to 512 neighbouring positions
- page_table: int32 [32, 8], P('dp'), may hold values from 0 to 7, each once within a row
- attn_gain: float32 [2048], replicated, may hold values from 0.1 to 1.9
- w_query: bfloat16 [2048, 1024], P(None, 'tensor'), may hold values from -0.125 to 0.125
- w_keyval: bfloat16 [2048, 512], replicated, may hold values from -0.125 to 0.125
- query_gain: float32 [64], replicated, may hold values from 0.1 to 1.9
- key_gain: float32 [64], replicated, may hold values from 0.1 to 1.9
- w_out: bfloat16 [1024, 2048], P('tensor'), may hold values from -0.1875 to 0.1875
- ffn_gain: float32 [2048], replicated, may hold values from 0.1 to 1.9
- w_gate: bfloat16 [2048, 5120], P(None, 'tensor'), may hold values from -0.125 to 0.125
- w_up: bfloat16 [2048, 5120], P(None, 'tensor'), may hold values from -0.125 to 0.125
- w_down: bfloat16 [5120, 2048], P('tensor'), may hold values from -0.078125 to 0.078125
Outputs:
- result: bfloat16 [32768, 2048], P('dp', 'tensor')
- kv_pages: bfloat16 [256, 128, 512], P('dp', None, 'tensor')
Inputs may be any that keep to these rules, and one draw needn't show every extreme that they name: deal[s, k] = g * 32 + j sends unit k of arrival block s to unit j of group g; every value occurs once; the units of one arrival block go to exactly 16 groups, 2 units to each. `seg_ids`: each row never falls; one prompt is one run of equal numbers. `page_table`: each row holds every page number once.
All inputs are finite; a program needn't handle non-finite values.
Results may differ from a plain program's by a relative error of at most 0.019.
Values may be sent and summed in bfloat16 or wider, within the bound.
No kernel may reach another device: no remote copies, remote signals or barrier semaphores. Data moves between devices by JAX's collectives and lax.ppermute only.
A program may use at most 128 MiB of HBM per device.

v0:
```python
import math
import jax
import jax.numpy as jnp
from jax import lax
from jax.sharding import PartitionSpec as P

HEAD = 64
KVH = 4
MOST = 2
PAGE = 128
EPS = 1e-06
THETA = 10000.0
BLOCK_ROWS = 512


def rms_scale(values, gain):
    values = values.astype(jnp.float32)
    mean_sq = jnp.mean(values * values, axis=-1, keepdims=True)
    return values * lax.rsqrt(mean_sq + EPS) * gain


def rope_tables(positions, width):
    half = width // 2
    inverse = THETA ** (-jnp.arange(half, dtype=jnp.float32) * 2.0 / width)
    angles = positions.astype(jnp.float32)[:, None] * inverse[None, :]
    return (jnp.cos(angles), jnp.sin(angles))


def rotate(values, cosine, sine):
    half = values.shape[-1] // 2
    first = values[..., :half]
    second = values[..., half:]
    cos_b = cosine[:, None, :]
    sin_b = sine[:, None, :]
    return jnp.concatenate(
        [first * cos_b - second * sin_b, second * cos_b + first * sin_b], axis=-1
    )


def segment_starts(seg_row):
    count = seg_row.shape[0]
    index = jnp.arange(count, dtype=jnp.int32)
    prior = jnp.concatenate([seg_row[:1] - 1, seg_row[:-1]])
    marks = jnp.where(seg_row != prior, index, 0)
    return lax.cummax(marks, axis=0)


def on_device(
    arrivals,
    deal,
    seg_ids,
    page_table,
    attn_gain,
    w_query,
    w_keyval,
    query_gain,
    key_gain,
    w_out,
    ffn_gain,
    w_gate,
    w_up,
    w_down,
):
    groups = lax.axis_size("dp")
    shards = lax.axis_size("tensor")
    tensor_rank = lax.axis_index("tensor")
    tok_grp = arrivals.shape[0]
    feat_part = arrivals.shape[1]
    units = deal.shape[1]
    unit_rows = tok_grp // units
    slot_count = groups * MOST
    width = unit_rows * feat_part
    dest_row = deal[0]
    target = dest_row // units
    position = dest_row % units
    unit_index = jnp.arange(units, dtype=jnp.int32)
    earlier = unit_index[:, None] > unit_index[None, :]
    same_target = target[:, None] == target[None, :]
    rank = jnp.sum(jnp.logical_and(earlier, same_target), axis=1)
    slot = target * MOST + rank
    send_hot = slot[None, :] == jnp.arange(slot_count, dtype=jnp.int32)[:, None]
    filled = jnp.any(send_hot, axis=1)
    slot_pos = jnp.where(filled, jnp.sum(jnp.where(send_hot, position[None, :], 0), axis=1), -1)
    send_matrix = send_hot.astype(jnp.bfloat16)
    packed = jnp.dot(
        send_matrix, arrivals.reshape(units, width), preferred_element_type=jnp.float32
    ).astype(jnp.bfloat16)
    received, recv_pos = (
        lax.all_to_all(
            packed.reshape(groups, MOST, width), "dp", split_axis=0, concat_axis=0, tiled=True
        ),
        lax.all_to_all(
            slot_pos.reshape(groups, MOST), "dp", split_axis=0, concat_axis=0, tiled=True
        ),
    )
    recv_matrix = (recv_pos.reshape(-1)[None, :] == unit_index[:, None]).astype(jnp.bfloat16)
    grouped = jnp.dot(
        recv_matrix, received.reshape(slot_count, width), preferred_element_type=jnp.float32
    ).astype(jnp.bfloat16)
    grouped = grouped.reshape(tok_grp, feat_part)
    full = lax.all_gather(grouped, "tensor", axis=1, tiled=True)
    normed = rms_scale(full, attn_gain).astype(jnp.bfloat16)
    seg_row = seg_ids[0]
    starts = segment_starts(seg_row)
    index = jnp.arange(tok_grp, dtype=jnp.int32)
    cosine, sine = rope_tables(index - starts, HEAD)
    q_heads = w_query.shape[1] // HEAD
    q_raw = jnp.dot(normed, w_query, preferred_element_type=jnp.float32).reshape(
        tok_grp, q_heads, HEAD
    )
    queries = rotate(rms_scale(q_raw, query_gain), cosine, sine).astype(jnp.bfloat16)
    kv_heads = max(1, KVH // shards)
    kv_first = tensor_rank * KVH // shards
    kv_weight = lax.dynamic_slice_in_dim(w_keyval, kv_first * 2 * HEAD, kv_heads * 2 * HEAD, 1)
    kv_raw = jnp.dot(normed, kv_weight, preferred_element_type=jnp.float32).reshape(
        tok_grp, kv_heads, 2, HEAD
    )
    keys = rotate(rms_scale(kv_raw[:, :, 0], key_gain), cosine, sine).astype(jnp.bfloat16)
    values = kv_raw[:, :, 1].astype(jnp.bfloat16)
    stacked = jnp.stack([keys, values], axis=2).reshape(tok_grp, kv_heads * 2 * HEAD)
    cache_cols = 2 * KVH * HEAD // shards
    offset = tensor_rank * cache_cols - kv_first * 2 * HEAD
    own_cache = lax.dynamic_slice_in_dim(stacked, offset, cache_cols, 1)
    pages = own_cache.reshape(tok_grp // PAGE, PAGE, cache_cols)
    kv_pages = jnp.zeros_like(pages).at[page_table[0]].set(pages)
    share = q_heads // kv_heads
    grouped_q = queries.reshape(tok_grp, kv_heads, share, HEAD)
    scale = 1.0 / math.sqrt(HEAD)
    block = min(BLOCK_ROWS, tok_grp)
    outputs = []
    for first in range(0, tok_grp, block):
        last = first + block
        scores = (
            jnp.einsum(
                "ikgd,jkd->kgij",
                grouped_q[first:last],
                keys[:last],
                preferred_element_type=jnp.float32,
            )
            * scale
        )
        query_rows = index[first:last]
        allowed = jnp.logical_and(
            query_rows[:, None] >= index[None, :last],
            starts[first:last][:, None] <= index[None, :last],
        )
        weights = jnp.where(allowed, jnp.exp(scores), 0.0)
        probs = (weights / jnp.sum(weights, axis=-1, keepdims=True)).astype(jnp.bfloat16)
        mixed = jnp.einsum(
            "kgij,jkd->ikgd", probs, values[:last], preferred_element_type=jnp.float32
        )
        outputs.append(mixed.astype(jnp.bfloat16).reshape(block, q_heads * HEAD))
    attended = jnp.concatenate(outputs, axis=0)
    attn_sum = lax.psum(
        jnp.dot(attended, w_out, preferred_element_type=jnp.float32).astype(jnp.bfloat16), "tensor"
    ).astype(jnp.float32)
    middle = (full.astype(jnp.float32) + attn_sum).astype(jnp.bfloat16)
    ffn_in = rms_scale(middle, ffn_gain).astype(jnp.bfloat16)
    gate = jnp.dot(ffn_in, w_gate, preferred_element_type=jnp.float32)
    upper = jnp.dot(ffn_in, w_up, preferred_element_type=jnp.float32)
    hidden = (jax.nn.silu(gate) * upper).astype(jnp.bfloat16)
    ffn_part = lax.psum_scatter(
        jnp.dot(hidden, w_down, preferred_element_type=jnp.float32).astype(jnp.bfloat16),
        "tensor",
        scatter_dimension=1,
        tiled=True,
    ).astype(jnp.float32)
    own_cols = lax.dynamic_slice_in_dim(middle, tensor_rank * feat_part, feat_part, 1)
    combined = (own_cols.astype(jnp.float32) + ffn_part).astype(jnp.bfloat16)
    back = jnp.dot(
        recv_matrix.T, combined.reshape(units, width), preferred_element_type=jnp.float32
    ).astype(jnp.bfloat16)
    returned = lax.all_to_all(
        back.reshape(groups, MOST, width), "dp", split_axis=0, concat_axis=0, tiled=True
    )
    result = jnp.dot(
        send_matrix.T, returned.reshape(slot_count, width), preferred_element_type=jnp.float32
    ).astype(jnp.bfloat16)
    return (result.reshape(tok_grp, feat_part), kv_pages)


def solution(mesh):
    return jax.shard_map(
        on_device,
        mesh=mesh,
        in_specs=(
            P("dp", "tensor"),
            P("dp", None),
            P("dp", None),
            P("dp", None),
            P(),
            P(None, "tensor"),
            P(),
            P(),
            P(),
            P("tensor", None),
            P(),
            P(None, "tensor"),
            P(None, "tensor"),
            P("tensor", None),
        ),
        out_specs=(P("dp", "tensor"), P("dp", None, "tensor")),
        check_vma=False,
    )
```

profile of v0, /device:TPU:65, one launch (start us, length us, event | category | flops | bytes accessed | tf_op | source)
XLA Modules:
  0.0 368.1 jit_solution(12057154090771228152)
XLA Ops:
  9.8 8.4 %all-to-all-start = ((s32[32,1,2]{2,1,0:T(1,128)}), s32[32,1,2]{2,1,0:T(1,128)S(1)}, u32[]{:S(2)}, u32[]{:S(2)}) async-start(s32[32,1,2]{2,1,0:T(1,128)} %bitcast.5), calls=%async_computation | async-start | bytes 32768 | tf_op jit(solution)/shard_map/all_to_all | solution.py:92
  18.2 1.3 reshape.501
  19.5 1.5 convolution_convert_fusion.1
  21.0 2.5 reshape.502
  23.5 1.7 all-to-all-done
  25.2 6.3 %all-to-all-start.1 = ((bf16[32,2,8192]{2,1,0:T(2,128)(2,1)}), bf16[32,2,8192]{2,1,0:T(2,128)(2,1)}, u32[]{:S(2)}, u32[]{:S(2)}) async-start(bf16[32,2,8192]{2,1,0:T(2,128)(2,1)} %reshape.502), calls=%async_computation.1 | async-start | bytes 2097152 | tf_op jit(solution)/shard_map/all_to_all | solution.py:89
  32.9 14.9 %all-to-all-done.1 = bf16[32,2,8192]{2,1,0:T(2,128)(2,1)} async-done(((bf16[32,2,8192]{2,1,0:T(2,128)(2,1)}), bf16[32,2,8192]{2,1,0:T(2,128)(2,1)}, u32[]{:S(2)}, u32[]{:S(2)}) %all-to-all-start.1) | async-done | bytes 1048608 | tf_op jit(solution)/shard_map/all_to_all | solution.py:89
  47.8 2.3 reshape.503
  50.1 1.5 convolution_convert_fusion.3
  51.6 1.0 reshape.504
  56.8 52.7 %all-gather.2.cloned.1.call-done = bf16[1024,2048]{1,0:T(8,128)(2,1)} async-done(((bf16[1024,256]{1,0:T(8,128)(2,1)}), bf16[1024,2048]{1,0:T(8,128)(2,1)}) %all-gather.2.cloned.1.call-update) | async-done | bytes 4194320 | tf_op jit(solution)/shard_map/all_gather | solution.py:101
  109.5 3.2 fusion.3
  113.0 2.6 fusion.19
  116.4 1.6 multiply_reduce_fusion
  119.0 1.1 fusion.7
  120.1 1.3 fusion.21
  122.5 3.3 convolution_convert_fusion.5
  126.0 116.0 %all-reduce.2.cloned.1.call-done = bf16[1024,2048]{1,0:T(8,128)(2,1)} async-done(((bf16[1024,2048]{1,0:T(8,128)(2,1)}), bf16[1024,2048]{1,0:T(8,128)(2,1)}) %all-reduce.2.cloned.1.call-update) | async-done | bytes 4194320 | tf_op jit(solution)/shard_map/psum | solution.py:154
  242.0 5.6 %fusion = (f32[1024]{0:T(1024)S(1)}, bf16[1024,2048]{1,0:T(8,128)(2,1)S(1)}) fusion(bf16[1024,2048]{1,0:T(8,128)(2,1)} %all-reduce.2.cloned.1.call-done, bf16[1024,2048]{1,0:T(8,128)(2,1)} %all-gather.2.cloned.1.call-done), kind=kLoop, calls=%fused_computation.10 | loop fusion | flops 14679040 | bytes 12587008 | tf_op jit(solution)/shard_map/reduce_sum | solution.py:18
  247.6 1.9 copy-done.2
  249.6 5.1 %fusion.13 = f32[1024,640]{1,0:T(8,128)} fusion(bf16[2048,640]{1,0:T(8,128)(2,1)S(1)} %copy-done.13, bf16[1024,2048]{1,0:T(8,128)(2,1)S(1)} %get-tuple-element.3, f32[2048]{0:T(1024)S(1)} %copy-done.17, f32[1024]{0:T(1024)S(1)} %add_rsqrt_fusion.1), kind=kOutput, calls=%fused_computation.31 | convolution fusion | flops 2692743168 | bytes 9449472 | tf_op jit(solution)/shard_map/dot_general | solution.py:159
  254.6 12.3 %convolution_convert_fusion.4 = bf16[1024,2048]{1,0:T(8,128)(2,1)} fusion(bf16[640,2048]{1,0:T(8,128)(2,1)S(1)} %copy-done, f32[1024,640]{1,0:T(8,128)} %fusion.13, bf16[2048,640]{1,0:T(8,128)(2,1)} %param.26, bf16[1024,2048]{1,0:T(8,128)(2,1)} %copy-done.2, f32[2048]{0:T(1024)S(1)} %copy-done.17, f32[1024]{0:T(1024)S(1)} %add_rsqrt_fusion.1), kind=kOutput, calls=%fused_computation.19 | convolution fusion | flops 5383127040 | bytes 16265216 | tf_op jit(solution)/shard_map/dot_general | solution.py:163
  267.0 59.3 %reduce-scatter.2.cloned.1.call-done = bf16[1024,256]{1,0:T(8,128)(2,1)} async-done(((bf16[1024,2048]{1,0:T(8,128)(2,1)}), bf16[1024,256]{1,0:T(8,128)(2,1)}) %reduce-scatter.2.cloned.1.call-update) | async-done | bytes 524304 | tf_op jit(solution)/shard_map/reduce_scatter | solution.py:162
  326.3 1.3 add_convert_fusion
  327.6 1.0 reshape.514
  328.7 2.5 convolution_convert_fusion
  331.2 2.5 reshape.515
  333.7 6.5 %all-to-all-start.2 = ((bf16[32,2,8192]{2,1,0:T(2,128)(2,1)}), bf16[32,2,8192]{2,1,0:T(2,128)(2,1)}, u32[]{:S(2)}, u32[]{:S(2)}) async-start(bf16[32,2,8192]{2,1,0:T(2,128)(2,1)} %reshape.515), calls=%async_computation.3 | async-start | bytes 2097152 | tf_op jit(solution)/shard_map/all_to_all | solution.py:173
  341.2 15.5 %all-to-all-done.2 = bf16[32,2,8192]{2,1,0:T(2,128)(2,1)} async-done(((bf16[32,2,8192]{2,1,0:T(2,128)(2,1)}), bf16[32,2,8192]{2,1,0:T(2,128)(2,1)}, u32[]{:S(2)}, u32[]{:S(2)}) %all-to-all-start.2) | async-done | bytes 1048608 | tf_op jit(solution)/shard_map/all_to_all | solution.py:173
  356.6 2.3 reshape.516
  358.9 1.6 convolution_convert_fusion.2
  360.5 1.0 reshape.517
  (87 shorter events, 11.5 us)
Async XLA Ops:
  7.2 247.5 %copy-start = (bf16[640,2048]{1,0:T(8,128)(2,1)S(1)}, bf16[640,2048]{1,0:T(8,128)(2,1)}, u32[]{:S(2)}) copy-start(bf16[640,2048]{1,0:T(8,128)(2,1)} %param.27) | copy-start | bytes 7864324
  9.8 15.4 %all-to-all-start = ((s32[32,1,2]{2,1,0:T(1,128)}), s32[32,1,2]{2,1,0:T(1,128)S(1)}, u32[]{:S(2)}, u32[]{:S(2)}) async-start(s32[32,1,2]{2,1,0:T(1,128)} %bitcast.5), calls=%async_computation | async-start | bytes 32768 | tf_op jit(solution)/shard_map/all_to_all | solution.py:92
  23.5 29.4 %copy-start.10 = (s32[1,1024]{1,0:T(1,128)S(1)}, s32[1,1024]{1,0:T(1,128)}, u32[]{:S(2)}) copy-start(s32[1,1024]{1,0:T(1,128)} %param.16) | copy-start | bytes 12292
  25.2 22.6 %all-to-all-start.1 = ((bf16[32,2,8192]{2,1,0:T(2,128)(2,1)}), bf16[32,2,8192]{2,1,0:T(2,128)(2,1)}, u32[]{:S(2)}, u32[]{:S(2)}) async-start(bf16[32,2,8192]{2,1,0:T(2,128)(2,1)} %reshape.502), calls=%async_computation.1 | async-start | bytes 2097152 | tf_op jit(solution)/shard_map/all_to_all | solution.py:89
  31.5 78.0 %all-gather.2.cloned.1.call-start = ((), (), s32[]{:S(2)}) async-start(), calls=%async_computation.4 | async-start | bytes 4718592 | tf_op jit(solution)/shard_map/all_gather | solution.py:101
  50.1 62.7 %copy-start.15 = (f32[2048]{0:T(1024)S(1)}, f32[2048]{0:T(1024)}, u32[]{:S(2)}) copy-start(f32[2048]{0:T(1024)} %param.18) | copy-start | bytes 24580
  52.6 189.4 %all-reduce.2.cloned.1.call-start = ((), (), s32[]{:S(2)}) async-start(), calls=%async_computation.5 | async-start | bytes 8388608 | tf_op jit(solution)/shard_map/psum | solution.py:154
  109.5 3.4 copy-start.1
  113.0 2.7 copy-start.11
  113.0 3.4 copy-start.14
  113.0 3.4 copy-start.16
  116.4 2.6 copy-start.6
  116.4 2.6 copy-start.8
  116.4 1.6 copy-start.12
  116.4 1.8 copy-start.5
  121.4 1.0 copy-start.4
  125.8 123.8 %copy-start.17 = (f32[2048]{0:T(1024)S(1)}, f32[2048]{0:T(1024)}, u32[]{:S(2)}) copy-start(f32[2048]{0:T(1024)} %param.24) | copy-start | bytes 24580
  125.8 200.5 %reduce-scatter.2.cloned.1.call-start = ((), (), s32[]{:S(2)}) async-start(), calls=%async_computation.6 | async-start | bytes 4718592 | tf_op jit(solution)/shard_map/reduce_scatter | solution.py:162
  242.0 7.5 %copy-start.13 = (bf16[2048,640]{1,0:T(8,128)(2,1)S(1)}, bf16[2048,640]{1,0:T(8,128)(2,1)}, u32[]{:S(2)}) copy-start(bf16[2048,640]{1,0:T(8,128)(2,1)} %param.25) | copy-start | bytes 7864324
  247.6 1.9 copy-start.2
  267.0 73.3 %copy-start.18 = (s32[1,8]{1,0:T(1,128)S(1)}, s32[1,8]{1,0:T(1,128)}, u32[]{:S(2)}) copy-start(s32[1,8]{1,0:T(1,128)} %param.17) | copy-start | bytes 100
  267.0 73.3 %copy-start.7 = (bf16[1024,1,32]{0,2,1:T(8,128)(2,1)S(1)}, bf16[1024,1,32]{0,2,1:T(8,128)(2,1)}, u32[]{:S(2)}) copy-start(bf16[1024,1,32]{0,2,1:T(8,128)(2,1)} %copy-done.6) | copy-start | bytes 196612
  267.0 73.3 %copy-start.9 = (bf16[1024,1,32]{0,2,1:T(8,128)(2,1)S(1)}, bf16[1024,1,32]{0,2,1:T(8,128)(2,1)}, u32[]{:S(2)}) copy-start(bf16[1024,1,32]{0,2,1:T(8,128)(2,1)} %copy-done.8) | copy-start | bytes 196612
  333.7 22.9 %all-to-all-start.2 = ((bf16[32,2,8192]{2,1,0:T(2,128)(2,1)}), bf16[32,2,8192]{2,1,0:T(2,128)(2,1)}, u32[]{:S(2)}, u32[]{:S(2)}) async-start(bf16[32,2,8192]{2,1,0:T(2,128)(2,1)} %reshape.515), calls=%async_computation.3 | async-start | bytes 2097152 | tf_op jit(solution)/shard_map/all_to_all | solution.py:173
  341.2 20.4 %copy-start.3 = (bf16[8,128,64]{1,2,0:T(8,128)(2,1)}, bf16[8,128,64]{1,2,0:T(8,128)(2,1)S(1)}, u32[]{:S(2)}) copy-start(bf16[8,128,64]{1,2,0:T(8,128)(2,1)S(1)} %scatter_fusion) | copy-start | bytes 393220
Sparse Core Ops, SparseCore 0:
  52.8 56.6 all-gather.1
  125.9 116.0 all-reduce.1
  267.1 59.1 reduce-scatter.1
where the time goes:
time: 369 us; the launch traced here: 368 us
  waiting for transfers between devices  260 us (70%)
  matrix products  35.9 us (10%)
  starting transfers between devices  21.8 us (6%)
  local copies, waits for them, and re-layouts  19.4 us (5%)
  other arithmetic  16.1 us (4%)
  between operations  14.9 us (4%)
    psum x1, waiting for transfers between devices, on_device(): lax.psum(jnp.dot(attended, w_out, preferred_element_type=jnp.float32).ast...  116 us
    reduce_scatter x1, waiting for transfers between devices, on_device(): lax.psum_scatter(jnp.dot(hidden, w_down, preferred_element_type=jnp.float...  59.3 us
    all_gather x1, waiting for transfers between devices, on_device(): full = lax.all_gather(grouped, 'tensor', axis=1, tiled=True)  52.7 us
    all_to_all x1, waiting for transfers between devices, on_device(): lax.all_to_all(back.reshape(groups, MOST, width), 'dp', split_axis=0, con...  15.5 us
    all_to_all x1, waiting for transfers between devices, on_device(): lax.all_to_all(packed.reshape(groups, MOST, width), 'dp', split_axis=0, c...  14.9 us
    dot_general x1, matrix products, on_device(): jnp.dot(hidden, w_down, preferred_element_type=jnp.float32)  12.3 us
    reduce_sum x3, other arithmetic, rms_scale(): mean_sq = jnp.mean(values * values, axis=-1, keepdims=True)  8.85 us
    all_to_all x1, starting transfers between devices, on_device(): lax.all_to_all(slot_pos.reshape(groups, MOST), 'dp', split_axis=0, concat...  8.39 us
  transfers between devices with their start and end apart: 6, of which 6 were waited for; matrix products, arithmetic and copies ran while one was open for 3% of the time, Pallas kernels for 0%

commit v1 on v0

--- a/solution.py
+++ b/solution.py
@@ -1,3 +1,4 @@
+import functools
 import math
 import jax
 import jax.numpy as jnp
@@ -11,6 +12,19 @@
 EPS = 1e-06
 THETA = 10000.0
 BLOCK_ROWS = 512
+
+
+def unite_sites(x_part, mesh_ax):
+    aux = jnp.concatenate(
+        lax.all_to_all(
+            jnp.stack([x_part for _ in range(lax.axis_size(mesh_ax))], axis=0), mesh_ax, 0, 0
+        ),
+        axis=1,
+    )
+    return aux
+
+
+create_the_paths = functools.partial(unite_sites, mesh_ax="tensor")
 
 
 def rms_scale(values, gain):
@@ -98,7 +112,7 @@
         recv_matrix, received.reshape(slot_count, width), preferred_element_type=jnp.float32
     ).astype(jnp.bfloat16)
     grouped = grouped.reshape(tok_grp, feat_part)
-    full = lax.all_gather(grouped, "tensor", axis=1, tiled=True)
+    full = create_the_paths(grouped)
     normed = rms_scale(full, attn_gain).astype(jnp.bfloat16)
     seg_row = seg_ids[0]
     starts = segment_starts(seg_row)

time: 369 us -> 421 us (1.14)
  local copies, waits for them, and re-layouts: 19.4 us -> 40.8 us
  waiting for transfers between devices: 260 us -> 275 us
  starting transfers between devices: 21.8 us -> 31 us
  other arithmetic: 16.1 us -> 24.1 us
    all_to_all x0 -> x1, waiting for transfers between devices: none -> 86.9 us  [unite_sites(): lax.all_to_all(jnp.stack([x_part for _ in range(lax.axis_size(mesh_ax))],...]
    all_gather x1 -> x0, waiting for transfers between devices: 52.7 us -> none  [on_device(): full = lax.all_gather(grouped, 'tensor', axis=1, tiled=True)]
    psum x1, waiting for transfers between devices: 116 us -> 97.1 us  [on_device(): lax.psum(jnp.dot(attended, w_out, preferred_element_type=jnp.float32).ast...]
    all_to_all x0 -> x1, starting transfers between devices: none -> 9.51 us  [unite_sites(): lax.all_to_all(jnp.stack([x_part for _ in range(lax.axis_size(mesh_ax))],...]
    convert_element_type x0 -> x1, local copies, waits for them, and re-layouts: none -> 9.17 us  [on_device(): middle = (full.astype(jnp.float32) + attn_sum).astype(jnp.bfloat16)]
    convert_element_type x0 -> x1, other arithmetic: none -> 6.45 us  [on_device(): middle = (full.astype(jnp.float32) + attn_sum).astype(jnp.bfloat16)]
    all_to_all x0 -> x1, local copies, waits for them, and re-layouts: none -> 6.44 us  [unite_sites(): lax.all_to_all(jnp.stack([x_part for _ in range(lax.axis_size(mesh_ax))],...]
  transfers between devices with their start and end apart: 6 -> 6, of which waited for: 6 -> 6; matrix products, arithmetic and copies ran while one was open for 3% -> 7% of each run, Pallas kernels for 0% -> 0%
where the time goes in v1:
time: 421 us; the launch traced here: 420 us
  waiting for transfers between devices  275 us (65%)
  local copies, waits for them, and re-layouts  40.8 us (10%)
  matrix products  34 us (8%)
  starting transfers between devices  31 us (7%)
  other arithmetic  24.1 us (6%)
  between operations  15.1 us (4%)
    psum x1, waiting for transfers between devices, on_device(): lax.psum(jnp.dot(attended, w_out, preferred_element_type=jnp.float32).ast...  97.1 us
    all_to_all x1, waiting for transfers between devices, unite_sites(): lax.all_to_all(jnp.stack([x_part for _ in range(lax.axis_size(mesh_ax))],...  86.9 us
    reduce_scatter x1, waiting for transfers between devices, on_device(): lax.psum_scatter(jnp.dot(hidden, w_down, preferred_element_type=jnp.float...  59.2 us
    all_to_all x1, waiting for transfers between devices, on_device(): lax.all_to_all(back.reshape(groups, MOST, width), 'dp', split_axis=0, con...  15.5 us
    all_to_all x1, waiting for transfers between devices, on_device(): lax.all_to_all(packed.reshape(groups, MOST, width), 'dp', split_axis=0, c...  14.9 us
    dot_general x1, matrix products, on_device(): jnp.dot(hidden, w_down, preferred_element_type=jnp.float32)  12.3 us
    all_to_all x1, starting transfers between devices, unite_sites(): lax.all_to_all(jnp.stack([x_part for _ in range(lax.axis_size(mesh_ax))],...  9.51 us
    reduce_sum x3, other arithmetic, rms_scale(): mean_sq = jnp.mean(values * values, axis=-1, keepdims=True)  9.31 us
  transfers between devices with their start and end apart: 6, of which 6 were waited for; matrix products, arithmetic and copies ran while one was open for 7% of the time, Pallas kernels for 0%

profile of v1, /device:TPU:65, one launch (start us, length us, event | category | flops | bytes accessed | tf_op | source)
XLA Modules:
  0.0 420.2 jit_solution(12551661456044844505)
XLA Ops:
  9.8 8.4 %all-to-all-start = ((s32[32,1,2]{2,1,0:T(1,128)}), s32[32,1,2]{2,1,0:T(1,128)S(1)}, u32[]{:S(2)}, u32[]{:S(2)}) async-start(s32[32,1,2]{2,1,0:T(1,128)} %bitcast.5), calls=%async_computation | async-start | bytes 32768 | tf_op jit(solution)/shard_map/all_to_all | solution.py:106
  18.2 1.3 reshape.528
  19.5 1.5 convolution_convert_fusion.1
  21.0 2.5 reshape.529
  23.5 1.7 all-to-all-done
  25.2 6.2 %all-to-all-start.1 = ((bf16[32,2,8192]{2,1,0:T(2,128)(2,1)}), bf16[32,2,8192]{2,1,0:T(2,128)(2,1)}, u32[]{:S(2)}, u32[]{:S(2)}) async-start(bf16[32,2,8192]{2,1,0:T(2,128)(2,1)} %reshape.529), calls=%async_computation.1 | async-start | bytes 2097152 | tf_op jit(solution)/shard_map/all_to_all | solution.py:103
  32.7 14.9 %all-to-all-done.1 = bf16[32,2,8192]{2,1,0:T(2,128)(2,1)} async-done(((bf16[32,2,8192]{2,1,0:T(2,128)(2,1)}), bf16[32,2,8192]{2,1,0:T(2,128)(2,1)}, u32[]{:S(2)}, u32[]{:S(2)}) %all-to-all-start.1) | async-done | bytes 1048608 | tf_op jit(solution)/shard_map/all_to_all | solution.py:103
  47.6 2.3 reshape.530
  49.9 2.3 convolution_convert_fusion.3
  52.2 1.3 stack_reshape.2
  53.5 2.2 stack.8
  55.7 9.5 %all-to-all-start.2 = ((bf16[8,1024,256]{2,1,0:T(8,128)(2,1)}), bf16[8,1024,256]{2,1,0:T(8,128)(2,1)}, u32[]{:S(2)}, u32[]{:S(2)}) async-start(bf16[8,1024,256]{2,1,0:T(8,128)(2,1)} %stack.8), calls=%async_computation.2 | async-start | bytes 8388608 | tf_op jit(solution)/shard_map/all_to_all | solution.py:19
  72.3 86.9 %all-to-all-done.2 = bf16[8,1024,256]{2,1,0:T(8,128)(2,1)} async-done(((bf16[8,1024,256]{2,1,0:T(8,128)(2,1)}), bf16[8,1024,256]{2,1,0:T(8,128)(2,1)}, u32[]{:S(2)}, u32[]{:S(2)}) %all-to-all-start.2) | async-done | bytes 4194336 | tf_op jit(solution)/shard_map/all_to_all | solution.py:19
  159.2 6.4 %copy.43 = bf16[8,1024,256]{1,2,0:T(8,128)(2,1)} copy(bf16[8,1024,256]{2,1,0:T(8,128)(2,1)} %all-to-all-done.2) | data formatting | bytes 8388608 | tf_op jit(solution)/shard_map/all_to_all | solution.py:19
  165.7 3.3 multiply_reduce_fusion
  174.8 1.3 fusion.13
  177.2 3.2 convolution_convert_fusion.5
  180.7 6.5 %convert_element_type.166 = f32[8,1024,256]{1,2,0:T(8,128)} convert(bf16[8,1024,256]{1,2,0:T(8,128)(2,1)} %copy.43) | non-fusion elementwise | flops 2097152 | bytes 12582912 | tf_op jit(solution)/shard_map/convert_element_type | solution.py:171
  187.2 9.2 %copy.56 = f32[1024,2048]{1,0:T(8,128)} copy(f32[1024,2048]{0,1:T(8,128)} %bitcast.148) | data formatting | bytes 16777216 | tf_op jit(solution)/shard_map/convert_element_type | solution.py:171
  196.4 97.1 %all-reduce.2.cloned.1.call-done = bf16[1024,2048]{1,0:T(8,128)(2,1)} async-done(((bf16[1024,2048]{1,0:T(8,128)(2,1)}), bf16[1024,2048]{1,0:T(8,128)(2,1)}) %all-reduce.2.cloned.1.call-update) | async-done | bytes 4194320 | tf_op jit(solution)/shard_map/psum | solution.py:168
  293.4 6.0 %fusion = (f32[1024]{0:T(1024)S(1)}, bf16[1024,2048]{1,0:T(8,128)(2,1)S(1)}) fusion(f32[1024,2048]{1,0:T(8,128)} %copy.56, bf16[1024,2048]{1,0:T(8,128)(2,1)} %all-reduce.2.cloned.1.call-done), kind=kLoop, calls=%fused_computation.7 | loop fusion | flops 12581888 | bytes 16781312 | tf_op jit(solution)/shard_map/reduce_sum | solution.py:32
  299.5 1.9 copy-done.2
  301.4 5.1 %fusion.9 = f32[1024,640]{1,0:T(8,128)} fusion(bf16[2048,640]{1,0:T(8,128)(2,1)S(1)} %copy-done.17, bf16[1024,2048]{1,0:T(8,128)(2,1)S(1)} %get-tuple-element.3, f32[2048]{0:T(1024)S(1)} %copy-done.18, f32[1024]{0:T(1024)S(1)} %add_rsqrt_fusion.1), kind=kOutput, calls=%fused_computation.28 | convolution fusion | flops 2692743168 | bytes 9449472 | tf_op jit(solution)/shard_map/dot_general | solution.py:173
  306.5 12.3 %convolution_convert_fusion.4 = bf16[1024,2048]{1,0:T(8,128)(2,1)} fusion(bf16[640,2048]{1,0:T(8,128)(2,1)S(1)} %copy-done, f32[1024,640]{1,0:T(8,128)} %fusion.9, bf16[2048,640]{1,0:T(8,128)(2,1)} %param.26, bf16[1024,2048]{1,0:T(8,128)(2,1)} %copy-done.2, f32[2048]{0:T(1024)S(1)} %copy-done.18, f32[1024]{0:T(1024)S(1)} %add_rsqrt_fusion.1), kind=kOutput, calls=%fused_computation.15 | convolution fusion | flops 5383127040 | bytes 16265216 | tf_op jit(solution)/shard_map/dot_general | solution.py:177
  318.8 59.2 %reduce-scatter.2.cloned.1.call-done = bf16[1024,256]{1,0:T(8,128)(2,1)} async-done(((bf16[1024,2048]{1,0:T(8,128)(2,1)}), bf16[1024,256]{1,0:T(8,128)(2,1)}) %reduce-scatter.2.cloned.1.call-update) | async-done | bytes 524304 | tf_op jit(solution)/shard_map/reduce_scatter | solution.py:176
  378.0 1.3 add_convert_fusion.1
  380.4 2.5 convolution_convert_fusion
  382.9 2.5 reshape.540
  385.4 6.7 %all-to-all-start.3 = ((bf16[32,2,8192]{2,1,0:T(2,128)(2,1)}), bf16[32,2,8192]{2,1,0:T(2,128)(2,1)}, u32[]{:S(2)}, u32[]{:S(2)}) async-start(bf16[32,2,8192]{2,1,0:T(2,128)(2,1)} %reshape.540), calls=%async_computation.4 | async-start | bytes 2097152 | tf_op jit(solution)/shard_map/all_to_all | solution.py:187
  393.0 15.5 %all-to-all-done.3 = bf16[32,2,8192]{2,1,0:T(2,128)(2,1)} async-done(((bf16[32,2,8192]{2,1,0:T(2,128)(2,1)}), bf16[32,2,8192]{2,1,0:T(2,128)(2,1)}, u32[]{:S(2)}, u32[]{:S(2)}) %all-to-all-start.3) | async-done | bytes 1048608 | tf_op jit(solution)/shard_map/all_to_all | solution.py:187
  408.5 2.3 reshape.541
  410.8 1.6 convolution_convert_fusion.2
  (97 shorter events, 20.3 us)
Async XLA Ops:
  7.2 299.3 %copy-start = (bf16[640,2048]{1,0:T(8,128)(2,1)S(1)}, bf16[640,2048]{1,0:T(8,128)(2,1)}, u32[]{:S(2)}) copy-start(bf16[640,2048]{1,0:T(8,128)(2,1)} %param.27) | copy-start | bytes 7864324
  9.8 15.4 %all-to-all-start = ((s32[32,1,2]{2,1,0:T(1,128)}), s32[32,1,2]{2,1,0:T(1,128)S(1)}, u32[]{:S(2)}, u32[]{:S(2)}) async-start(s32[32,1,2]{2,1,0:T(1,128)} %bitcast.5), calls=%async_computation | async-start | bytes 32768 | tf_op jit(solution)/shard_map/all_to_all | solution.py:106
  25.2 22.4 %all-to-all-start.1 = ((bf16[32,2,8192]{2,1,0:T(2,128)(2,1)}), bf16[32,2,8192]{2,1,0:T(2,128)(2,1)}, u32[]{:S(2)}, u32[]{:S(2)}) async-start(bf16[32,2,8192]{2,1,0:T(2,128)(2,1)} %reshape.529), calls=%async_computation.1 | async-start | bytes 2097152 | tf_op jit(solution)/shard_map/all_to_all | solution.py:103
  55.7 9.5 %copy-start.13 = (s32[1,1024]{1,0:T(1,128)S(1)}, s32[1,1024]{1,0:T(1,128)}, u32[]{:S(2)}) copy-start(s32[1,1024]{1,0:T(1,128)} %param.16) | copy-start | bytes 12292
  55.7 11.2 %copy-start.14 = (f32[2048]{0:T(1024)S(1)}, f32[2048]{0:T(1024)}, u32[]{:S(2)}) copy-start(f32[2048]{0:T(1024)} %param.18) | copy-start | bytes 24580
  55.7 11.2 %copy-start.5 = (bf16[2048,128]{1,0:T(8,128)(2,1)S(1)}, bf16[2048,128]{1,0:T(8,128)(2,1)}, u32[]{:S(2)}) copy-start(bf16[2048,128]{1,0:T(8,128)(2,1)} %param.19) | copy-start | bytes 1572868
  55.7 103.5 %all-to-all-start.2 = ((bf16[8,1024,256]{2,1,0:T(8,128)(2,1)}), bf16[8,1024,256]{2,1,0:T(8,128)(2,1)}, u32[]{:S(2)}, u32[]{:S(2)}) async-start(bf16[8,1024,256]{2,1,0:T(8,128)(2,1)} %stack.8), calls=%async_computation.2 | async-start | bytes 8388608 | tf_op jit(solution)/shard_map/all_to_all | solution.py:19
  65.2 228.2 %all-reduce.2.cloned.1.call-start = ((), (), s32[]{:S(2)}) async-start(), calls=%async_computation.5 | async-start | bytes 8388608 | tf_op jit(solution)/shard_map/psum | solution.py:168
  165.7 3.4 copy-start.1
  169.1 1.1 copy-start.7
  170.2 1.0 copy-start.6
  170.9 1.1 copy-start.15
  171.0 1.7 copy-start.16
  171.2 1.7 copy-start.8
  172.7 2.1 copy-start.9
  172.7 2.1 copy-start.11
  176.2 1.0 copy-start.4
  180.5 197.6 %reduce-scatter.2.cloned.1.call-start = ((), (), s32[]{:S(2)}) async-start(), calls=%async_computation.6 | async-start | bytes 4718592 | tf_op jit(solution)/shard_map/reduce_scatter | solution.py:176
  196.4 105.0 %copy-start.18 = (f32[2048]{0:T(1024)S(1)}, f32[2048]{0:T(1024)}, u32[]{:S(2)}) copy-start(f32[2048]{0:T(1024)} %param.24) | copy-start | bytes 24580
  293.4 7.9 %copy-start.17 = (bf16[2048,640]{1,0:T(8,128)(2,1)S(1)}, bf16[2048,640]{1,0:T(8,128)(2,1)}, u32[]{:S(2)}) copy-start(bf16[2048,640]{1,0:T(8,128)(2,1)} %param.25) | copy-start | bytes 7864324
  299.4 1.9 copy-start.2
  318.8 73.3 %copy-start.19 = (s32[1,8]{1,0:T(1,128)S(1)}, s32[1,8]{1,0:T(1,128)}, u32[]{:S(2)}) copy-start(s32[1,8]{1,0:T(1,128)} %param.17) | copy-start | bytes 100
  318.8 73.3 %copy-start.10 = (bf16[1024,1,32]{0,2,1:T(8,128)(2,1)S(1)}, bf16[1024,1,32]{0,2,1:T(8,128)(2,1)}, u32[]{:S(2)}) copy-start(bf16[1024,1,32]{0,2,1:T(8,128)(2,1)} %copy-done.9) | copy-start | bytes 196612
  318.8 73.3 %copy-start.12 = (bf16[1024,1,32]{0,2,1:T(8,128)(2,1)S(1)}, bf16[1024,1,32]{0,2,1:T(8,128)(2,1)}, u32[]{:S(2)}) copy-start(bf16[1024,1,32]{0,2,1:T(8,128)(2,1)} %copy-done.11) | copy-start | bytes 196612
  385.4 23.0 %all-to-all-start.3 = ((bf16[32,2,8192]{2,1,0:T(2,128)(2,1)}), bf16[32,2,8192]{2,1,0:T(2,128)(2,1)}, u32[]{:S(2)}, u32[]{:S(2)}) async-start(bf16[32,2,8192]{2,1,0:T(2,128)(2,1)} %reshape.540), calls=%async_computation.4 | async-start | bytes 2097152 | tf_op jit(solution)/shard_map/all_to_all | solution.py:187
  393.0 20.4 %copy-start.3 = (bf16[8,128,64]{1,2,0:T(8,128)(2,1)}, bf16[8,128,64]{1,2,0:T(8,128)(2,1)S(1)}, u32[]{:S(2)}) copy-start(bf16[8,128,64]{1,2,0:T(8,128)(2,1)S(1)} %scatter_fusion) | copy-start | bytes 393220
Sparse Core Ops, SparseCore 0:
  180.6 112.7 all-reduce.1
  318.9 59.0 reduce-scatter.1
